TPU v7x, 32 devices: a whole 2x2x4 slice. The times are simulated.
32 devices in a mesh: ri: 4 (over z), ao: 8 (over y, x, core).
Axes of the slice: x: 2, y: 2, z: 4, core: 2. Of those that a mesh axis runs over, the one named last changes fastest.
Arguments:
- tensor: bfloat16 [512, 256, 256], P('ri', 'ao'), may hold values from -0.5 to 0.5
- live_blocks: int32 [8, 8, 8], P('ri', 'ao'), may hold values 0 or 1
- occ_density: bfloat16 [256, 256], P('ao'), may hold values from -0.375 to 0.375
- virt_density: bfloat16 [256, 256], P('ao'), may hold values from -0.375 to 0.375
- occ_mask: int32 [8, 8], P('ao'), may hold values 0 or 1
- virt_mask: int32 [8, 8], P('ao'), may hold values 0 or 1
- pair_slots: int32 [8, 8], P('ao'), may hold values from 0 to 7, as said below
Outputs:
- polar: float32 [512, 512], P('ri', 'ao')
Inputs may be any that keep to these rules, and one draw needn't show every extreme that they name: pair_slots[b, 0] = b, and the 8 entries of a row are different AO blocks.
All inputs are finite; a program needn't handle non-finite values. No bound on the sum of `live_blocks` or of `occ_mask` or of `virt_mask` on one device may be relied on, other than what follows from the above.
Results may differ from a plain program's by a relative error of at most 0.0041.
Values may be sent and summed in bfloat16 or wider, within the bound.
No kernel may reach another device: no remote copies, remote signals or barrier semaphores. Data moves between devices by JAX's collectives and lax.ppermute only.
A program may use at most 192 MiB of HBM per device.

v0:
```python
import jax
import jax.numpy as jnp
from jax import lax
from jax.sharding import PartitionSpec as P

BS = 32
KS = 8
RB = 64


def shifted(block, axis, distance):
    devices = range(lax.axis_size(axis))
    route = [((i - distance) % len(devices), i) for i in devices]
    return lax.ppermute(block, axis, route)


def screen_density(density, block_mask):
    own_blocks = block_mask.shape[0]
    all_blocks = block_mask.shape[1]
    shaped = density.reshape(own_blocks, BS, all_blocks, BS)
    keeper = block_mask.astype(density.dtype)[:, None, :, None]
    return (shaped * keeper).reshape(density.shape)


def pick_slots(pair_slots, stacked, first_block):
    own_blocks = stacked.shape[1] // BS
    block_ids = first_block + jnp.arange(own_blocks, dtype=jnp.int32)
    matches = (pair_slots[:, :, None] == block_ids[None, None, :]).astype(jnp.bfloat16)
    shaped = stacked.reshape(2, own_blocks, BS, stacked.shape[2])
    return jnp.einsum("bkc,tcjn->tbkjn", matches, shaped, preferred_element_type=jnp.float32)


def per_device(tensor, live_blocks, occ_density, virt_density, occ_mask, virt_mask, pair_slots):
    own_rows = tensor.shape[0]
    own_width = tensor.shape[1]
    own_blocks = own_width // BS
    groups = live_blocks.shape[0]
    keeper = live_blocks.astype(jnp.bfloat16)[:, None, :, None, :, None]
    tensor_eff = (tensor.reshape(groups, RB, own_blocks, BS, KS, BS) * keeper).reshape(tensor.shape)
    stacked = jnp.stack(
        [screen_density(occ_density, occ_mask), screen_density(virt_density, virt_mask)]
    )
    ao_total = stacked.shape[2]
    cycle_size = lax.axis_size("ao")
    position = lax.axis_index("ao")

    def visit(turn_index, state):
        current, gathered_rows = state
        current = shifted(current, "ao", 1)
        source = (position - turn_index + cycle_size) % cycle_size
        return (current, gathered_rows + pick_slots(pair_slots, current, source * own_blocks))

    start_pick = pick_slots(pair_slots, stacked, position * own_blocks)
    unused, picked = lax.fori_loop(1, cycle_size, visit, (stacked, start_pick))
    picked = picked.astype(jnp.bfloat16)
    occ_rows = picked[0]
    virt_rows = picked[1]
    span_cols = min(128, ao_total)
    piece_count = ao_total // span_cols
    tensor_five = tensor_eff.reshape(own_rows, own_blocks, BS, KS, BS)
    occ_pieces = occ_rows.reshape(own_blocks, KS, BS, piece_count, span_cols)

    def occ_piece(piece_index):
        columns = lax.dynamic_index_in_dim(occ_pieces, piece_index, 3, keepdims=False)
        product = jnp.einsum(
            "pbikj,bkjl->lbip", tensor_five, columns, preferred_element_type=jnp.float32
        )
        return product.astype(jnp.bfloat16).reshape(span_cols, own_width, own_rows)

    half_occ = lax.map(occ_piece, jnp.arange(piece_count, dtype=jnp.int32)).reshape(
        ao_total, own_width, own_rows
    )
    half_occ_local = lax.all_to_all(half_occ, "ao", split_axis=0, concat_axis=1, tiled=True)

    def virt_piece(source_rows, piece_index):
        columns = lax.dynamic_slice_in_dim(virt_rows, piece_index * span_cols, span_cols, 3)
        product = jnp.einsum(
            "qbikj,bkjn->qbin", source_rows, columns, preferred_element_type=jnp.float32
        )
        return product.astype(jnp.bfloat16).reshape(source_rows.shape[0], own_width, span_cols)

    all_tensor = lax.all_gather(tensor_eff, "ri", axis=0, tiled=True)
    kept_rows = all_tensor.shape[0] // cycle_size
    source_rows = all_tensor
    polar_source_rows = source_rows.reshape(kept_rows * lax.axis_size("ao"), own_blocks, BS, KS, BS)

    def add_piece(piece_index, running):
        virt_part = virt_piece(polar_source_rows, piece_index)
        occ_part = lax.dynamic_slice_in_dim(half_occ_local, piece_index * span_cols, span_cols, 1)
        return running + jnp.einsum(
            "qln,lnp->qp", virt_part, occ_part, preferred_element_type=jnp.float32
        )

    polar_block = lax.psum_scatter(
        lax.fori_loop(
            0,
            piece_count,
            add_piece,
            jnp.zeros((polar_source_rows.shape[0], own_rows), jnp.float32),
        ),
        "ao",
        scatter_dimension=0,
        tiled=True,
    )
    return polar_block.T


def solution(mesh):
    placed = (
        P("ri", "ao", None),
        P("ri", "ao", None),
        P("ao", None),
        P("ao", None),
        P("ao", None),
        P("ao", None),
        P("ao", None),
    )
    return jax.shard_map(
        per_device, mesh=mesh, in_specs=placed, out_specs=P("ri", "ao"), check_vma=False
    )
```

profile of v0, /device:TPU:0, one launch (start us, length us, event | category | flops | bytes accessed | tf_op | source)
XLA Modules:
  0.0 228.5 jit_solution(457382478721264577)
XLA Ops:
  6.5 0.7 convert_element_type.41
  7.2 0.1 copy.51
  7.3 0.1 mul.93
  7.5 0.1 mul.94
  7.6 0.1 copy.41
  7.7 3.1 %broadcast_multiply_fusion.1 = bf16[128,32,256]{2,1,0:T(8,128)(2,1)} fusion(bf16[128,32,256]{2,1,0:T(8,128)(2,1)} %param.13, bf16[128,256]{1,0:T(8,128)(2,1)S(1)} %copy.41), kind=kLoop, calls=%fused_computation.23 | loop fusion | flops 1048576 | bytes 4259840 | tf_op jit(solution)/shard_map/mul | solution.py:39
  10.9 1.6 copy-done.1
  12.5 3.1 %copy.43 = bf16[128,32,256]{0,2,1:T(8,128)(2,1)} copy(bf16[128,32,256]{2,1,0:T(8,128)(2,1)S(1)} %copy-done.1) | data formatting | bytes 4194304 | tf_op args[0]
  16.0 0.1 multiply_bitcast_fusion
  16.1 32.0 %while.41 = (s32[]{:T(128)}, bf16[2,32,256]{2,1,0:T(8,128)(2,1)S(1)}, f32[2,1,8,32,256]{4,3,2,1,0:T(8,128)S(1)}, s32[]{:T(128)}, s32[1,8]{1,0:T(1,128)S(1)}, /*index=5*/s32[]{:T(128)}, s32[]{:T(128)}, s32[]{:T(128)}, s32[]{:T(128)}) while((s32[]{:T(128)}, bf16[2,32,256]{2,1,0:T(8,128)(2,1)S(1)}, f32[2,1,8,32,256]{4,3,2,1,0:T(8,128)S(1)}, ...), condition=%wide.region_1.2_spmd, body=%wide.region_0.1_spmd.sunk | while | flops 278559 | bytes 1409390 | solution.py:54
  16.1 0.5 collective-permute-start
  16.6 4.5 %collective-permute-done = bf16[2,32,256]{2,1,0:T(8,128)(2,1)S(1)} collective-permute-done((bf16[2,32,256]{2,1,0:T(8,128)(2,1)S(1)}, bf16[2,32,256]{2,1,0:T(8,128)(2,1)S(1)}, u32[]{:S(2)}, u32[]{:S(2)}) %collective-permute-start) | collective-permute-done | bytes 32800 | tf_op jit(solution)/shard_map/while/body/eval_jaxpr/ppermute | solution.py:14
  21.1 0.1 bitcast_add_fusion.2
  21.3 4.2 %collective-permute-done = bf16[2,32,256]{2,1,0:T(8,128)(2,1)S(1)} collective-permute-done((bf16[2,32,256]{2,1,0:T(8,128)(2,1)S(1)}, bf16[2,32,256]{2,1,0:T(8,128)(2,1)S(1)}, u32[]{:S(2)}, u32[]{:S(2)}) %collective-permute-start) | collective-permute-done | bytes 32800 | tf_op jit(solution)/shard_map/while/body/eval_jaxpr/ppermute | solution.py:14
  25.5 0.1 bitcast_add_fusion.2
  25.8 4.2 %collective-permute-done = bf16[2,32,256]{2,1,0:T(8,128)(2,1)S(1)} collective-permute-done((bf16[2,32,256]{2,1,0:T(8,128)(2,1)S(1)}, bf16[2,32,256]{2,1,0:T(8,128)(2,1)S(1)}, u32[]{:S(2)}, u32[]{:S(2)}) %collective-permute-start) | collective-permute-done | bytes 32800 | tf_op jit(solution)/shard_map/while/body/eval_jaxpr/ppermute | solution.py:14
  30.0 0.1 bitcast_add_fusion.2
  30.3 4.2 %collective-permute-done = bf16[2,32,256]{2,1,0:T(8,128)(2,1)S(1)} collective-permute-done((bf16[2,32,256]{2,1,0:T(8,128)(2,1)S(1)}, bf16[2,32,256]{2,1,0:T(8,128)(2,1)S(1)}, u32[]{:S(2)}, u32[]{:S(2)}) %collective-permute-start) | collective-permute-done | bytes 32800 | tf_op jit(solution)/shard_map/while/body/eval_jaxpr/ppermute | solution.py:14
  34.5 0.1 bitcast_add_fusion.2
  34.8 4.2 %collective-permute-done = bf16[2,32,256]{2,1,0:T(8,128)(2,1)S(1)} collective-permute-done((bf16[2,32,256]{2,1,0:T(8,128)(2,1)S(1)}, bf16[2,32,256]{2,1,0:T(8,128)(2,1)S(1)}, u32[]{:S(2)}, u32[]{:S(2)}) %collective-permute-start) | collective-permute-done | bytes 32800 | tf_op jit(solution)/shard_map/while/body/eval_jaxpr/ppermute | solution.py:14
  39.0 0.1 bitcast_add_fusion.2
  39.2 4.2 %collective-permute-done = bf16[2,32,256]{2,1,0:T(8,128)(2,1)S(1)} collective-permute-done((bf16[2,32,256]{2,1,0:T(8,128)(2,1)S(1)}, bf16[2,32,256]{2,1,0:T(8,128)(2,1)S(1)}, u32[]{:S(2)}, u32[]{:S(2)}) %collective-permute-start) | collective-permute-done | bytes 32800 | tf_op jit(solution)/shard_map/while/body/eval_jaxpr/ppermute | solution.py:14
  43.4 0.1 bitcast_add_fusion.2
  43.7 4.2 %collective-permute-done = bf16[2,32,256]{2,1,0:T(8,128)(2,1)S(1)} collective-permute-done((bf16[2,32,256]{2,1,0:T(8,128)(2,1)S(1)}, bf16[2,32,256]{2,1,0:T(8,128)(2,1)S(1)}, u32[]{:S(2)}, u32[]{:S(2)}) %collective-permute-start) | collective-permute-done | bytes 32800 | tf_op jit(solution)/shard_map/while/body/eval_jaxpr/ppermute | solution.py:14
  47.9 0.1 bitcast_add_fusion.2
  48.3 1.7 broadcast_multiply_fusion
  50.1 12.4 %while.42 = (s32[]{:T(128)}, bf16[2,128,32,128]{3,2,1,0:T(8,128)(2,1)}, s32[2]{0:T(128)S(1)}, bf16[1,8,32,2,128]{4,2,1,3,0:T(8,128)(2,1)S(1)}, bf16[128,1,32,8,3...) while((s32[]{:T(128)}, bf16[2,128,32,128]{3,2,1,0:T(8,128)(2,1)}, s32[2]{0:T(128)S(1)}, ...), condition=%wide.region_3.4_spmd, body=%wide.region_2.3_spmd.sunk | while | flops 268959744 | bytes 22085836 | solution.py:70
  50.1 0.6 dynamic_slice.40
  52.7 0.5 fusion.52
  53.1 1.1 copy-done.3
  54.3 0.7 copy_dynamic-update-slice_fusion.2
  55.0 1.3 copy-done.4
  56.3 0.6 dynamic_slice.40
  58.9 0.5 fusion.52
  59.3 1.1 copy-done.3
  60.4 0.7 copy_dynamic-update-slice_fusion.2
  61.2 1.3 copy-done.4
  62.5 3.6 %all-to-all-start = ((bf16[256,32,128]{2,1,0:T(8,128)(2,1)}), bf16[256,32,128]{2,1,0:T(8,128)(2,1)S(1)}, u32[]{:S(2)}, u32[]{:S(2)}) async-start(bf16[256,32,128]{2,1,0:T(8,128)(2,1)} %bitcast.132), calls=%async_computation | async-start | bytes 4194304 | tf_op jit(solution)/shard_map/all_to_all | solution.py:73
  66.2 26.5 %all-to-all-done = bf16[256,32,128]{2,1,0:T(8,128)(2,1)S(1)} async-done(((bf16[256,32,128]{2,1,0:T(8,128)(2,1)}), bf16[256,32,128]{2,1,0:T(8,128)(2,1)S(1)}, u32[]{:S(2)}, u32[]{:S(2)}) %all-to-all-start) | async-done | bytes 2097184 | tf_op jit(solution)/shard_map/all_to_all | solution.py:73
  92.7 1.3 copy-done.2
  94.0 2.2 copy.47
  96.3 67.1 %all-gather.2.cloned.1.call-done = bf16[512,32,256]{2,1,0:T(8,128)(2,1)} async-done(((bf16[128,32,256]{2,1,0:T(8,128)(2,1)}), bf16[512,32,256]{2,1,0:T(8,128)(2,1)}) %all-gather.2.cloned.1.call-update) | async-done | bytes 8388624 | tf_op jit(solution)/shard_map/all_gather | solution.py:82
  163.4 13.8 %copy.42 = bf16[512,32,256]{0,2,1:T(8,128)(2,1)} copy(bf16[512,32,256]{2,1,0:T(8,128)(2,1)} %all-gather.2.cloned.1.call-done) | data formatting | bytes 16777216 | tf_op jit(solution)/shard_map/all_gather | solution.py:82
  177.2 11.8 %while.43 = (s32[]{:T(128)}, f32[512,128]{1,0:T(8,128)S(1)}, bf16[1,8,32,256]{3,2,1,0:T(8,128)(2,1)S(1)}, bf16[512,1,32,8,32]{0,4,3,2,1:T(8,128)(2,1)}, bf16[32,...) while((s32[]{:T(128)}, f32[512,128]{1,0:T(8,128)S(1)}, ...), condition=%wide.region_5.6_spmd.clone, body=%wide.region_4.5_spmd.clone.sunk | while | flops 1612840960 | bytes 10028700 | solution.py:95
  177.2 5.9 %fusion.57 = f32[512,128]{1,0:T(8,128)S(1)} fusion(bf16[512,1,32,8,32]{0,4,3,2,1:T(8,128)(2,1)} %get-tuple-element.511, bf16[32,256,128]{2,1,0:T(8,128)(2,1)S(1)} %get-tuple-element.512, s32[]{:T(128)S(6)} %select_n.38, f32[512,128]{1,0:T(8,128)S(1)} %get-tuple-element.500, pred[]{:T(512)S(6)} %compare.4, ...), kind=kOutput, calls=%fused_computation.17.clone.1 | convolution fusion | flops 1612840960 | bytes 10028544 | tf_op jit(solution)/shard_map/while/body/eval_jaxpr/qln,lnp->qp/dot_general | solution.py:90
  183.1 5.9 %fusion.57 = f32[512,128]{1,0:T(8,128)S(1)} fusion(bf16[512,1,32,8,32]{0,4,3,2,1:T(8,128)(2,1)} %get-tuple-element.511, bf16[32,256,128]{2,1,0:T(8,128)(2,1)S(1)} %get-tuple-element.512, s32[]{:T(128)S(6)} %select_n.38, f32[512,128]{1,0:T(8,128)S(1)} %get-tuple-element.500, pred[]{:T(512)S(6)} %compare.4, ...), kind=kOutput, calls=%fused_computation.17.clone.1 | convolution fusion | flops 1612840960 | bytes 10028544 | tf_op jit(solution)/shard_map/while/body/eval_jaxpr/qln,lnp->qp/dot_general | solution.py:90
  189.0 0.7 copy-done
  189.7 32.0 %reduce-scatter.2.cloned.1.call-done = f32[64,128]{1,0:T(8,128)} async-done(((f32[512,128]{1,0:T(8,128)}), f32[64,128]{1,0:T(8,128)}) %reduce-scatter.2.cloned.1.call-update) | async-done | bytes 32784 | tf_op jit(solution)/shard_map/reduce_scatter | solution.py:94
  (66 shorter events, 1.2 us)
Async XLA Ops:
  6.5 156.8 %all-gather.2.cloned.1.call-start = ((), (), s32[]{:S(2)}) async-start(), calls=%async_computation.2 | async-start | bytes 10485760 | tf_op jit(solution)/shard_map/all_gather | solution.py:82
  10.8 1.6 copy-start.1
  12.4 3.1 %copy-start.7 = (s32[1,8]{1,0:T(1,128)S(1)}, s32[1,8]{1,0:T(1,128)}, u32[]{:S(2)}) copy-start(s32[1,8]{1,0:T(1,128)} %param.18) | copy-start | bytes 100
  12.4 3.3 %copy-start.8 = (s32[1,8]{1,0:T(1,128)S(1)}, s32[1,8]{1,0:T(1,128)}, u32[]{:S(2)}) copy-start(s32[1,8]{1,0:T(1,128)} %param.17) | copy-start | bytes 100
  12.4 3.5 %copy-start.5 = (bf16[32,256]{1,0:T(8,128)(2,1)S(1)}, bf16[32,256]{1,0:T(8,128)(2,1)}, u32[]{:S(2)}) copy-start(bf16[32,256]{1,0:T(8,128)(2,1)} %param.16) | copy-start | bytes 49156
  12.4 3.5 %copy-start.6 = (bf16[32,256]{1,0:T(8,128)(2,1)S(1)}, bf16[32,256]{1,0:T(8,128)(2,1)}, u32[]{:S(2)}) copy-start(bf16[32,256]{1,0:T(8,128)(2,1)} %param.15) | copy-start | bytes 49156
  12.4 3.5 %copy-start.9 = (s32[1,8]{1,0:T(1,128)S(1)}, s32[1,8]{1,0:T(1,128)}, u32[]{:S(2)}) copy-start(s32[1,8]{1,0:T(1,128)} %param.19) | copy-start | bytes 100
  16.1 5.0 %collective-permute-start = (bf16[2,32,256]{2,1,0:T(8,128)(2,1)S(1)}, bf16[2,32,256]{2,1,0:T(8,128)(2,1)S(1)}, u32[]{:S(2)}, u32[]{:S(2)}) collective-permute-start(bf16[2,32,256]{2,1,0:T(8,128)(2,1)S(1)} %get-tuple-element.449), channel_id=1, source_target_pairs={{7,0},{0,1},{1,2},{2,3},{3,4},{4,5},{5,6},{6,7},{15,8},{8,9},{9,10... | collective-permute-start | bytes 98312 | tf_op jit(solution)/shard_map/while/body/eval_jaxpr/ppermute | solution.py:14
  21.2 4.3 %collective-permute-start = (bf16[2,32,256]{2,1,0:T(8,128)(2,1)S(1)}, bf16[2,32,256]{2,1,0:T(8,128)(2,1)S(1)}, u32[]{:S(2)}, u32[]{:S(2)}) collective-permute-start(bf16[2,32,256]{2,1,0:T(8,128)(2,1)S(1)} %get-tuple-element.449), channel_id=1, source_target_pairs={{7,0},{0,1},{1,2},{2,3},{3,4},{4,5},{5,6},{6,7},{15,8},{8,9},{9,10... | collective-permute-start | bytes 98312 | tf_op jit(solution)/shard_map/while/body/eval_jaxpr/ppermute | solution.py:14
  25.7 4.3 %collective-permute-start = (bf16[2,32,256]{2,1,0:T(8,128)(2,1)S(1)}, bf16[2,32,256]{2,1,0:T(8,128)(2,1)S(1)}, u32[]{:S(2)}, u32[]{:S(2)}) collective-permute-start(bf16[2,32,256]{2,1,0:T(8,128)(2,1)S(1)} %get-tuple-element.449), channel_id=1, source_target_pairs={{7,0},{0,1},{1,2},{2,3},{3,4},{4,5},{5,6},{6,7},{15,8},{8,9},{9,10... | collective-permute-start | bytes 98312 | tf_op jit(solution)/shard_map/while/body/eval_jaxpr/ppermute | solution.py:14
  30.2 4.3 %collective-permute-start = (bf16[2,32,256]{2,1,0:T(8,128)(2,1)S(1)}, bf16[2,32,256]{2,1,0:T(8,128)(2,1)S(1)}, u32[]{:S(2)}, u32[]{:S(2)}) collective-permute-start(bf16[2,32,256]{2,1,0:T(8,128)(2,1)S(1)} %get-tuple-element.449), channel_id=1, source_target_pairs={{7,0},{0,1},{1,2},{2,3},{3,4},{4,5},{5,6},{6,7},{15,8},{8,9},{9,10... | collective-permute-start | bytes 98312 | tf_op jit(solution)/shard_map/while/body/eval_jaxpr/ppermute | solution.py:14
  34.7 4.3 %collective-permute-start = (bf16[2,32,256]{2,1,0:T(8,128)(2,1)S(1)}, bf16[2,32,256]{2,1,0:T(8,128)(2,1)S(1)}, u32[]{:S(2)}, u32[]{:S(2)}) collective-permute-start(bf16[2,32,256]{2,1,0:T(8,128)(2,1)S(1)} %get-tuple-element.449), channel_id=1, source_target_pairs={{7,0},{0,1},{1,2},{2,3},{3,4},{4,5},{5,6},{6,7},{15,8},{8,9},{9,10... | collective-permute-start | bytes 98312 | tf_op jit(solution)/shard_map/while/body/eval_jaxpr/ppermute | solution.py:14
  39.1 4.3 %collective-permute-start = (bf16[2,32,256]{2,1,0:T(8,128)(2,1)S(1)}, bf16[2,32,256]{2,1,0:T(8,128)(2,1)S(1)}, u32[]{:S(2)}, u32[]{:S(2)}) collective-permute-start(bf16[2,32,256]{2,1,0:T(8,128)(2,1)S(1)} %get-tuple-element.449), channel_id=1, source_target_pairs={{7,0},{0,1},{1,2},{2,3},{3,4},{4,5},{5,6},{6,7},{15,8},{8,9},{9,10... | collective-permute-start | bytes 98312 | tf_op jit(solution)/shard_map/while/body/eval_jaxpr/ppermute | solution.py:14
  43.6 4.3 %collective-permute-start = (bf16[2,32,256]{2,1,0:T(8,128)(2,1)S(1)}, bf16[2,32,256]{2,1,0:T(8,128)(2,1)S(1)}, u32[]{:S(2)}, u32[]{:S(2)}) collective-permute-start(bf16[2,32,256]{2,1,0:T(8,128)(2,1)S(1)} %get-tuple-element.449), channel_id=1, source_target_pairs={{7,0},{0,1},{1,2},{2,3},{3,4},{4,5},{5,6},{6,7},{15,8},{8,9},{9,10... | collective-permute-start | bytes 98312 | tf_op jit(solution)/shard_map/while/body/eval_jaxpr/ppermute | solution.py:14
  52.6 1.6 copy-start.3
  55.0 1.3 copy-start.4
  58.9 1.6 copy-start.3
  61.2 1.3 copy-start.4
  62.5 30.2 %all-to-all-start = ((bf16[256,32,128]{2,1,0:T(8,128)(2,1)}), bf16[256,32,128]{2,1,0:T(8,128)(2,1)S(1)}, u32[]{:S(2)}, u32[]{:S(2)}) async-start(bf16[256,32,128]{2,1,0:T(8,128)(2,1)} %bitcast.132), calls=%async_computation | async-start | bytes 4194304 | tf_op jit(solution)/shard_map/all_to_all | solution.py:73
  66.1 155.6 %reduce-scatter.2.cloned.1.call-start = ((), (), s32[]{:S(2)}) async-start(), calls=%async_computation.3 | async-start | bytes 294912 | tf_op jit(solution)/shard_map/reduce_scatter | solution.py:94
  92.7 1.3 copy-start.2
  189.0 0.7 copy-start
Sparse Core Ops, SparseCore 0:
  11.0 152.3 all-gather.1
  189.8 31.8 reduce-scatter.1
where the time goes:
time: 229 us
  waiting for transfers between devices  155 us (68%)
  local copies, waits for them, and re-layouts  31.3 us (14%)
  between operations  13.6 us (6%)
  matrix products  12.7 us (6%)
  other arithmetic  6.8 us (3%)
  starting transfers between devices  4.5 us (2%)
  loops' own time  4.39 us (2%)
    all_gather x1, waiting for transfers between devices, per_device(): all_tensor = lax.all_gather(tensor_eff, 'ri', axis=0, tiled=True)  67.1 us
    reduce_scatter x1, waiting for transfers between devices, per_device(): lax.psum_scatter(lax.fori_loop(0, piece_count, add_piece, jnp.zeros((pola...  32 us
    ppermute x7, waiting for transfers between devices, shifted(): return lax.ppermute(block, axis, route)  29.6 us
    all_to_all x1, waiting for transfers between devices, per_device(): lax.all_to_all(half_occ, 'ao', split_axis=0, concat_axis=1, tiled=True)  26.5 us
    all_gather x1, local copies, waits for them, and re-layouts, per_device(): all_tensor = lax.all_gather(tensor_eff, 'ri', axis=0, tiled=True)  13.8 us
    dot_general x2, matrix products, add_piece(): jnp.einsum('qln,lnp->qp', virt_part, occ_part, preferred_element_type=jnp...  11.8 us
    unnamed x17, local copies, waits for them, and re-layouts  6.7 us
    while x15, local copies, waits for them, and re-layouts  4.9 us
  transfers between devices with their start and end apart: 10, of which 10 were waited for; matrix products, arithmetic and copies ran while one was open for 5% of the time, Pallas kernels for 0%

commit v1 on v0

--- a/solution.py
+++ b/solution.py
@@ -79,7 +79,26 @@
         )
         return product.astype(jnp.bfloat16).reshape(source_rows.shape[0], own_width, span_cols)
 
-    all_tensor = lax.all_gather(tensor_eff, "ri", axis=0, tiled=True)
+    devices_2, index, extent = (lax.axis_size("ri"), lax.axis_index("ri"), tensor_eff.shape[0])
+    right = [(i_2, (i_2 + 1) % devices_2) for i_2 in range(devices_2)]
+    downward = [(i_2, (i_2 - 1) % devices_2) for i_2 in range(devices_2)]
+    out = jnp.zeros(
+        (*tensor_eff.shape[:0], devices_2 * extent, *tensor_eff.shape[0 + 1 :]), tensor_eff.dtype
+    )
+    out = lax.dynamic_update_slice_in_dim(out, tensor_eff, index * extent, axis=0)
+    from_left = from_right = tensor_eff
+    halfway = devices_2 // 2
+    for step in range(1, halfway + 1):
+        from_left = lax.ppermute(from_left, "ri", right)
+        out = lax.dynamic_update_slice_in_dim(
+            out, from_left, (index - step) % devices_2 * extent, axis=0
+        )
+        if step < devices_2 - halfway:
+            from_right = lax.ppermute(from_right, "ri", downward)
+            out = lax.dynamic_update_slice_in_dim(
+                out, from_right, (index + step) % devices_2 * extent, axis=0
+            )
+    all_tensor = out
     kept_rows = all_tensor.shape[0] // cycle_size
     source_rows = all_tensor
     polar_source_rows = source_rows.reshape(kept_rows * lax.axis_size("ao"), own_blocks, BS, KS, BS)

time: 229 us -> 213 us (0.930)
  waiting for transfers between devices: 155 us -> 120 us
  local copies, waits for them, and re-layouts: 31.3 us -> 45 us
  starting transfers between devices: 4.5 us -> 9.16 us
    all_gather x1 -> x0, waiting for transfers between devices: 67.1 us -> none  [per_device(): all_tensor = lax.all_gather(tensor_eff, 'ri', axis=0, tiled=True)]
    ppermute x0 -> x3, waiting for transfers between devices: none -> 41.9 us  [the longest x2 35.9 us: per_device(): from_left = lax.ppermute(from_left, 'ri', right)]
    all_gather x1 -> x0, local copies, waits for them, and re-layouts: 13.8 us -> none  [per_device(): all_tensor = lax.all_gather(tensor_eff, 'ri', axis=0, tiled=True)]
    ppermute x0 -> x3, local copies, waits for them, and re-layouts: none -> 13.7 us  [the longest x2 9.14 us: per_device(): from_left = lax.ppermute(from_left, 'ri', right)]
    all_to_all x1, waiting for transfers between devices: 26.5 us -> 16.1 us  [per_device(): lax.all_to_all(half_occ, 'ao', split_axis=0, concat_axis=1, tiled=True)]
    dynamic_update_slice x0 -> x4, local copies, waits for them, and re-layouts: none -> 9.75 us  [the longest x2 6.55 us: per_device(): lax.dynamic_update_slice_in_dim(out, from_left, (index - step) % devices_...]
    ppermute x0 -> x3, starting transfers between devices: none -> 5.11 us  [the longest x2 3.08 us: per_device(): from_left = lax.ppermute(from_left, 'ri', right)]
    while x15 -> x7, local copies, waits for them, and re-layouts: 4.9 us -> 0.03 us
  transfers between devices with their start and end apart: 10 -> 12, of which waited for: 10 -> 11; matrix products, arithmetic and copies ran while one was open for 5% -> 18% of each run, Pallas kernels for 0% -> 0%
where the time goes in v1:
time: 213 us; the launch traced here: 212 us
  waiting for transfers between devices  120 us (56%)
  local copies, waits for them, and re-layouts  45 us (21%)
  between operations  13.6 us (6%)
  matrix products  12.7 us (6%)
  starting transfers between devices  9.16 us (4%)
  other arithmetic  6.87 us (3%)
  loops' own time  4.38 us (2%)
    ppermute x2, waiting for transfers between devices, per_device(): from_left = lax.ppermute(from_left, 'ri', right)  35.9 us
    reduce_scatter x1, waiting for transfers between devices, per_device(): lax.psum_scatter(lax.fori_loop(0, piece_count, add_piece, jnp.zeros((pola...  33.1 us
    ppermute x7, waiting for transfers between devices, shifted(): return lax.ppermute(block, axis, route)  29.3 us
    all_to_all x1, waiting for transfers between devices, per_device(): lax.all_to_all(half_occ, 'ao', split_axis=0, concat_axis=1, tiled=True)  16.1 us
    dot_general x2, matrix products, add_piece(): jnp.einsum('qln,lnp->qp', virt_part, occ_part, preferred_element_type=jnp...  11.8 us
    ppermute x2, local copies, waits for them, and re-layouts, per_device(): from_left = lax.ppermute(from_left, 'ri', right)  9.14 us
    dynamic_update_slice x2, local copies, waits for them, and re-layouts, per_device(): lax.dynamic_update_slice_in_dim(out, from_left, (index - step) % devices_...  6.55 us
    ppermute x1, waiting for transfers between devices, per_device(): from_right = lax.ppermute(from_right, 'ri', downward)  5.98 us
  transfers between devices with their start and end apart: 12, of which 11 were waited for; matrix products, arithmetic and copies ran while one was open for 18% of the time, Pallas kernels for 0%

profile of v1, /device:TPU:0, one launch (start us, length us, event | category | flops | bytes accessed | tf_op | source)
XLA Modules:
  0.0 212.2 jit_solution(5514306746655585732)
XLA Ops:
  6.5 0.7 convert_element_type.41
  7.7 3.2 %broadcast_multiply_fusion.1 = bf16[128,32,256]{2,1,0:T(8,128)(2,1)} fusion(bf16[128,32,256]{2,1,0:T(8,128)(2,1)} %param.13, bf16[128,256]{1,0:T(8,128)(2,1)S(1)} %copy.29), kind=kLoop, calls=%fused_computation.23 | loop fusion | flops 1048576 | bytes 4259840 | tf_op jit(solution)/shard_map/mul | solution.py:39
  10.9 3.0 %collective-permute-start.1 = (bf16[128,32,256]{2,1,0:T(8,128)(2,1)}, bf16[128,32,256]{2,1,0:T(8,128)(2,1)}, u32[]{:S(2)}, u32[]{:S(2)}) collective-permute-start(bf16[128,32,256]{2,1,0:T(8,128)(2,1)} %broadcast_multiply_fusion.1), channel_id=1, source_target_pairs={{0,8},{8,16},{16,24},{24,0},{1,9},{9,17},{17,25},{25,1},{2,10},{10... | collective-permute-start | bytes 6291464 | tf_op jit(solution)/shard_map/ppermute | solution.py:92
  14.0 2.0 collective-permute-start.2
  16.0 3.1 %copy.34 = bf16[128,32,256]{0,2,1:T(8,128)(2,1)} copy(bf16[128,32,256]{2,1,0:T(8,128)(2,1)S(1)} %copy-done.1) | data formatting | bytes 4194304 | tf_op args[0]
  19.6 31.3 %while.41 = (s32[]{:T(128)}, bf16[2,32,256]{2,1,0:T(8,128)(2,1)S(1)}, f32[2,1,8,32,256]{4,3,2,1,0:T(8,128)S(1)}, s32[]{:T(128)}, s32[1,8]{1,0:T(1,128)S(1)}, /*index=5*/s32[]{:T(128)}, s32[]{:T(128)}, s32[]{:T(128)}, s32[]{:T(128)}) while((s32[]{:T(128)}, bf16[2,32,256]{2,1,0:T(8,128)(2,1)S(1)}, f32[2,1,8,32,256]{4,3,2,1,0:T(8,128)S(1)}, ...), condition=%wide.region_1.2_spmd, body=%wide.region_0.1_spmd.sunk | while | flops 278559 | bytes 1409390 | solution.py:54
  19.7 4.2 %collective-permute-done = bf16[2,32,256]{2,1,0:T(8,128)(2,1)S(1)} collective-permute-done((bf16[2,32,256]{2,1,0:T(8,128)(2,1)S(1)}, bf16[2,32,256]{2,1,0:T(8,128)(2,1)S(1)}, u32[]{:S(2)}, u32[]{:S(2)}) %collective-permute-start) | collective-permute-done | bytes 32800 | tf_op jit(solution)/shard_map/while/body/eval_jaxpr/ppermute | solution.py:14
  23.9 0.1 bitcast_add_fusion.2
  24.2 4.2 %collective-permute-done = bf16[2,32,256]{2,1,0:T(8,128)(2,1)S(1)} collective-permute-done((bf16[2,32,256]{2,1,0:T(8,128)(2,1)S(1)}, bf16[2,32,256]{2,1,0:T(8,128)(2,1)S(1)}, u32[]{:S(2)}, u32[]{:S(2)}) %collective-permute-start) | collective-permute-done | bytes 32800 | tf_op jit(solution)/shard_map/while/body/eval_jaxpr/ppermute | solution.py:14
  28.4 0.1 bitcast_add_fusion.2
  28.6 4.2 %collective-permute-done = bf16[2,32,256]{2,1,0:T(8,128)(2,1)S(1)} collective-permute-done((bf16[2,32,256]{2,1,0:T(8,128)(2,1)S(1)}, bf16[2,32,256]{2,1,0:T(8,128)(2,1)S(1)}, u32[]{:S(2)}, u32[]{:S(2)}) %collective-permute-start) | collective-permute-done | bytes 32800 | tf_op jit(solution)/shard_map/while/body/eval_jaxpr/ppermute | solution.py:14
  32.8 0.1 bitcast_add_fusion.2
  33.1 4.2 %collective-permute-done = bf16[2,32,256]{2,1,0:T(8,128)(2,1)S(1)} collective-permute-done((bf16[2,32,256]{2,1,0:T(8,128)(2,1)S(1)}, bf16[2,32,256]{2,1,0:T(8,128)(2,1)S(1)}, u32[]{:S(2)}, u32[]{:S(2)}) %collective-permute-start) | collective-permute-done | bytes 32800 | tf_op jit(solution)/shard_map/while/body/eval_jaxpr/ppermute | solution.py:14
  37.3 0.1 bitcast_add_fusion.2
  37.6 4.2 %collective-permute-done = bf16[2,32,256]{2,1,0:T(8,128)(2,1)S(1)} collective-permute-done((bf16[2,32,256]{2,1,0:T(8,128)(2,1)S(1)}, bf16[2,32,256]{2,1,0:T(8,128)(2,1)S(1)}, u32[]{:S(2)}, u32[]{:S(2)}) %collective-permute-start) | collective-permute-done | bytes 32800 | tf_op jit(solution)/shard_map/while/body/eval_jaxpr/ppermute | solution.py:14
  41.8 0.1 bitcast_add_fusion.2
  42.0 4.2 %collective-permute-done = bf16[2,32,256]{2,1,0:T(8,128)(2,1)S(1)} collective-permute-done((bf16[2,32,256]{2,1,0:T(8,128)(2,1)S(1)}, bf16[2,32,256]{2,1,0:T(8,128)(2,1)S(1)}, u32[]{:S(2)}, u32[]{:S(2)}) %collective-permute-start) | collective-permute-done | bytes 32800 | tf_op jit(solution)/shard_map/while/body/eval_jaxpr/ppermute | solution.py:14
  46.2 0.1 bitcast_add_fusion.2
  46.5 4.2 %collective-permute-done = bf16[2,32,256]{2,1,0:T(8,128)(2,1)S(1)} collective-permute-done((bf16[2,32,256]{2,1,0:T(8,128)(2,1)S(1)}, bf16[2,32,256]{2,1,0:T(8,128)(2,1)S(1)}, u32[]{:S(2)}, u32[]{:S(2)}) %collective-permute-start) | collective-permute-done | bytes 32800 | tf_op jit(solution)/shard_map/while/body/eval_jaxpr/ppermute | solution.py:14
  50.7 0.1 bitcast_add_fusion.2
  51.2 1.7 broadcast_multiply_fusion
  52.9 9.4 %while.42 = (s32[]{:T(128)}, bf16[2,128,32,128]{3,2,1,0:T(8,128)(2,1)}, s32[2]{0:T(128)S(1)}, bf16[1,8,32,2,128]{4,2,1,3,0:T(8,128)(2,1)S(1)}, bf16[128,1,32,8,3...) while((s32[]{:T(128)}, bf16[2,128,32,128]{3,2,1,0:T(8,128)(2,1)}, s32[2]{0:T(128)S(1)}, ...), condition=%wide.region_3.4_spmd, body=%wide.region_2.3_spmd.sunk | while | flops 268959744 | bytes 5309063 | solution.py:70
  52.9 0.6 dynamic_slice.40
  55.5 0.5 fusion.52
  55.9 1.7 copy_dynamic-update-slice_fusion.2
  57.6 0.6 dynamic_slice.40
  60.2 0.5 fusion.52
  60.6 1.6 copy_dynamic-update-slice_fusion.2
  62.3 3.6 %all-to-all-start = ((bf16[256,32,128]{2,1,0:T(8,128)(2,1)}), bf16[256,32,128]{2,1,0:T(8,128)(2,1)S(1)}, u32[]{:S(2)}, u32[]{:S(2)}) async-start(bf16[256,32,128]{2,1,0:T(8,128)(2,1)} %bitcast.23), calls=%async_computation | async-start | bytes 4194304 | tf_op jit(solution)/shard_map/all_to_all | solution.py:73
  66.0 4.5 %copy.30 = bf16[128,32,256]{0,2,1:T(8,128)(2,1)} copy(bf16[128,32,256]{2,1,0:T(8,128)(2,1)} %broadcast_multiply_fusion.1) | data formatting | bytes 4194304 | tf_op jit(solution)/shard_map/mul | solution.py:39
  70.6 4.2 %broadcast_in_dim.21 = bf16[512,32,256]{0,2,1:T(8,128)(2,1)} broadcast(bf16[]{:T(256)} %constant.121.clone.1), dimensions={} | broadcast | bytes 8388610 | tf_op jit(solution)/shard_map/broadcast_in_dim | solution.py:85
  74.8 1.6 constant_dynamic-update-slice_fusion.3
  76.4 16.1 %all-to-all-done = bf16[256,32,128]{2,1,0:T(8,128)(2,1)S(1)} async-done(((bf16[256,32,128]{2,1,0:T(8,128)(2,1)}), bf16[256,32,128]{2,1,0:T(8,128)(2,1)S(1)}, u32[]{:S(2)}, u32[]{:S(2)}) %all-to-all-start) | async-done | bytes 2097184 | tf_op jit(solution)/shard_map/all_to_all | solution.py:73
  92.5 1.3 copy-done.2
  93.8 2.2 %copy.38 = bf16[32,8,32,128]{3,2,1,0:T(8,128)(2,1)S(1)} copy(bf16[32,8,32,128]{3,2,0,1:T(8,128)(2,1)} %bitcast.129) | data formatting | bytes 4194304 | tf_op jit(solution)/shard_map/all_to_all | solution.py:73
  96.0 4.5 %copy.31 = bf16[128,32,256]{0,2,1:T(8,128)(2,1)} copy(bf16[128,32,256]{2,1,0:T(8,128)(2,1)} %collective-permute-done.1) | data formatting | bytes 4194304 | tf_op jit(solution)/shard_map/ppermute | solution.py:92
  100.5 6.0 %collective-permute-done.2 = bf16[128,32,256]{2,1,0:T(8,128)(2,1)} collective-permute-done((bf16[128,32,256]{2,1,0:T(8,128)(2,1)}, bf16[128,32,256]{2,1,0:T(8,128)(2,1)}, u32[]{:S(2)}, u32[]{:S(2)}) %collective-permute-start.2) | collective-permute-done | bytes 2097184 | tf_op jit(solution)/shard_map/ppermute | solution.py:97
  106.5 4.6 %copy.32 = bf16[128,32,256]{0,2,1:T(8,128)(2,1)} copy(bf16[128,32,256]{2,1,0:T(8,128)(2,1)} %collective-permute-done.2) | data formatting | bytes 4194304 | tf_op jit(solution)/shard_map/ppermute | solution.py:97
  111.1 3.3 %constant_dynamic-update-slice_fusion.2 = bf16[512,32,256]{0,2,1:T(8,128)(2,1)} fusion(bf16[512,32,256]{0,2,1:T(8,128)(2,1)} %constant_dynamic-update-slice_fusion.3, bf16[128,32,256]{0,2,1:T(8,128)(2,1)} %copy.31, s32[]{:T(128)S(6)} %select_n.58), kind=kLoop, calls=%fused_computation.32 | loop fusion | bytes 4194308 | tf_op jit(solution)/shard_map/dynamic_update_slice | solution.py:93
  114.4 1.6 constant_dynamic-update-slice_fusion.1
  116.0 35.9 %collective-permute-done.3 = bf16[128,32,256]{2,1,0:T(8,128)(2,1)} collective-permute-done((bf16[128,32,256]{2,1,0:T(8,128)(2,1)}, bf16[128,32,256]{2,1,0:T(8,128)(2,1)}, u32[]{:S(2)}, u32[]{:S(2)}) %collective-permute-start.3) | collective-permute-done | bytes 2097184 | tf_op jit(solution)/shard_map/ppermute | solution.py:92
  151.9 4.6 %copy.33 = bf16[128,32,256]{0,2,1:T(8,128)(2,1)} copy(bf16[128,32,256]{2,1,0:T(8,128)(2,1)} %collective-permute-done.3) | data formatting | bytes 4194304 | tf_op jit(solution)/shard_map/ppermute | solution.py:92
  156.5 3.2 %constant_dynamic-update-slice_fusion = bf16[512,32,256]{0,2,1:T(8,128)(2,1)} fusion(bf16[512,32,256]{0,2,1:T(8,128)(2,1)} %constant_dynamic-update-slice_fusion.1, bf16[128,32,256]{0,2,1:T(8,128)(2,1)} %copy.33, s32[]{:T(128)S(6)} %select_n.62), kind=kLoop, calls=%fused_computation.30 | loop fusion | bytes 4194308 | tf_op jit(solution)/shard_map/dynamic_update_slice | solution.py:93
  159.7 11.8 %while.43 = (s32[]{:T(128)}, f32[512,128]{1,0:T(8,128)S(1)}, bf16[1,8,32,256]{3,2,1,0:T(8,128)(2,1)S(1)}, bf16[512,1,32,8,32]{0,4,3,2,1:T(8,128)(2,1)}, bf16[32,...) while((s32[]{:T(128)}, f32[512,128]{1,0:T(8,128)S(1)}, ...), condition=%wide.region_5.6_spmd.clone, body=%wide.region_4.5_spmd.clone.sunk | while | flops 1612840960 | bytes 10028692 | solution.py:114
  159.7 5.9 %fusion.57 = f32[512,128]{1,0:T(8,128)S(1)} fusion(bf16[512,1,32,8,32]{0,4,3,2,1:T(8,128)(2,1)} %get-tuple-element.496, bf16[32,256,128]{2,1,0:T(8,128)(2,1)S(1)} %get-tuple-element.497, s32[]{:T(128)S(6)} %select_n.69, f32[512,128]{1,0:T(8,128)S(1)} %get-tuple-element.485, pred[]{:T(512)S(6)} %compare.7, ...), kind=kOutput, calls=%fused_computation.17.clone.1 | convolution fusion | flops 1612840960 | bytes 10028544 | tf_op jit(solution)/shard_map/while/body/eval_jaxpr/qln,lnp->qp/dot_general | solution.py:109
  165.6 5.9 %fusion.57 = f32[512,128]{1,0:T(8,128)S(1)} fusion(bf16[512,1,32,8,32]{0,4,3,2,1:T(8,128)(2,1)} %get-tuple-element.496, bf16[32,256,128]{2,1,0:T(8,128)(2,1)S(1)} %get-tuple-element.497, s32[]{:T(128)S(6)} %select_n.69, f32[512,128]{1,0:T(8,128)S(1)} %get-tuple-element.485, pred[]{:T(512)S(6)} %compare.7, ...), kind=kOutput, calls=%fused_computation.17.clone.1 | convolution fusion | flops 1612840960 | bytes 10028544 | tf_op jit(solution)/shard_map/while/body/eval_jaxpr/qln,lnp->qp/dot_general | solution.py:109
  171.5 0.7 copy-done
  172.2 33.1 %reduce-scatter.2.cloned.1.call-done = f32[64,128]{1,0:T(8,128)} async-done(((f32[512,128]{1,0:T(8,128)}), f32[64,128]{1,0:T(8,128)}) %reduce-scatter.2.cloned.1.call-update) | async-done | bytes 32784 | tf_op jit(solution)/shard_map/reduce_scatter | solution.py:113
  (73 shorter events, 1.9 us)
Async XLA Ops:
  7.7 8.3 %copy-start.1 = (bf16[128,32,256]{2,1,0:T(8,128)(2,1)S(1)}, bf16[128,32,256]{2,1,0:T(8,128)(2,1)}, u32[]{:S(2)}) copy-start(bf16[128,32,256]{2,1,0:T(8,128)(2,1)} %param.13) | copy-start | bytes 6291460
  10.9 55.0 %collective-permute-start.1 = (bf16[128,32,256]{2,1,0:T(8,128)(2,1)}, bf16[128,32,256]{2,1,0:T(8,128)(2,1)}, u32[]{:S(2)}, u32[]{:S(2)}) collective-permute-start(bf16[128,32,256]{2,1,0:T(8,128)(2,1)} %broadcast_multiply_fusion.1), channel_id=1, source_target_pairs={{0,8},{8,16},{16,24},{24,0},{1,9},{9,17},{17,25},{25,1},{2,10},{10... | collective-permute-start | bytes 6291464 | tf_op jit(solution)/shard_map/ppermute | solution.py:92
  14.0 92.6 %collective-permute-start.2 = (bf16[128,32,256]{2,1,0:T(8,128)(2,1)}, bf16[128,32,256]{2,1,0:T(8,128)(2,1)}, u32[]{:S(2)}, u32[]{:S(2)}) collective-permute-start(bf16[128,32,256]{2,1,0:T(8,128)(2,1)} %broadcast_multiply_fusion.1), channel_id=1, source_target_pairs={{0,24},{8,0},{16,8},{24,16},{1,25},{9,1},{17,9},{25,17},{2,26},{10... | collective-permute-start | bytes 6291464 | tf_op jit(solution)/shard_map/ppermute | solution.py:97
  16.0 3.1 %copy-start.7 = (s32[1,8]{1,0:T(1,128)S(1)}, s32[1,8]{1,0:T(1,128)}, u32[]{:S(2)}) copy-start(s32[1,8]{1,0:T(1,128)} %param.18) | copy-start | bytes 100
  16.0 3.3 %copy-start.8 = (s32[1,8]{1,0:T(1,128)S(1)}, s32[1,8]{1,0:T(1,128)}, u32[]{:S(2)}) copy-start(s32[1,8]{1,0:T(1,128)} %param.17) | copy-start | bytes 100
  16.0 3.4 %copy-start.5 = (bf16[32,256]{1,0:T(8,128)(2,1)S(1)}, bf16[32,256]{1,0:T(8,128)(2,1)}, u32[]{:S(2)}) copy-start(bf16[32,256]{1,0:T(8,128)(2,1)} %param.16) | copy-start | bytes 49156
  16.0 3.4 %copy-start.6 = (bf16[32,256]{1,0:T(8,128)(2,1)S(1)}, bf16[32,256]{1,0:T(8,128)(2,1)}, u32[]{:S(2)}) copy-start(bf16[32,256]{1,0:T(8,128)(2,1)} %param.15) | copy-start | bytes 49156
  16.0 3.5 %copy-start.9 = (s32[1,8]{1,0:T(1,128)S(1)}, s32[1,8]{1,0:T(1,128)}, u32[]{:S(2)}) copy-start(s32[1,8]{1,0:T(1,128)} %param.19) | copy-start | bytes 100
  19.6 4.3 %collective-permute-start = (bf16[2,32,256]{2,1,0:T(8,128)(2,1)S(1)}, bf16[2,32,256]{2,1,0:T(8,128)(2,1)S(1)}, u32[]{:S(2)}, u32[]{:S(2)}) collective-permute-start(bf16[2,32,256]{2,1,0:T(8,128)(2,1)S(1)} %get-tuple-element.434), channel_id=1, source_target_pairs={{7,0},{0,1},{1,2},{2,3},{3,4},{4,5},{5,6},{6,7},{15,8},{8,9},{9,10... | collective-permute-start | bytes 98312 | tf_op jit(solution)/shard_map/while/body/eval_jaxpr/ppermute | solution.py:14
  24.1 4.3 %collective-permute-start = (bf16[2,32,256]{2,1,0:T(8,128)(2,1)S(1)}, bf16[2,32,256]{2,1,0:T(8,128)(2,1)S(1)}, u32[]{:S(2)}, u32[]{:S(2)}) collective-permute-start(bf16[2,32,256]{2,1,0:T(8,128)(2,1)S(1)} %get-tuple-element.434), channel_id=1, source_target_pairs={{7,0},{0,1},{1,2},{2,3},{3,4},{4,5},{5,6},{6,7},{15,8},{8,9},{9,10... | collective-permute-start | bytes 98312 | tf_op jit(solution)/shard_map/while/body/eval_jaxpr/ppermute | solution.py:14
  28.5 4.3 %collective-permute-start = (bf16[2,32,256]{2,1,0:T(8,128)(2,1)S(1)}, bf16[2,32,256]{2,1,0:T(8,128)(2,1)S(1)}, u32[]{:S(2)}, u32[]{:S(2)}) collective-permute-start(bf16[2,32,256]{2,1,0:T(8,128)(2,1)S(1)} %get-tuple-element.434), channel_id=1, source_target_pairs={{7,0},{0,1},{1,2},{2,3},{3,4},{4,5},{5,6},{6,7},{15,8},{8,9},{9,10... | collective-permute-start | bytes 98312 | tf_op jit(solution)/shard_map/while/body/eval_jaxpr/ppermute | solution.py:14
  33.0 4.3 %collective-permute-start = (bf16[2,32,256]{2,1,0:T(8,128)(2,1)S(1)}, bf16[2,32,256]{2,1,0:T(8,128)(2,1)S(1)}, u32[]{:S(2)}, u32[]{:S(2)}) collective-permute-start(bf16[2,32,256]{2,1,0:T(8,128)(2,1)S(1)} %get-tuple-element.434), channel_id=1, source_target_pairs={{7,0},{0,1},{1,2},{2,3},{3,4},{4,5},{5,6},{6,7},{15,8},{8,9},{9,10... | collective-permute-start | bytes 98312 | tf_op jit(solution)/shard_map/while/body/eval_jaxpr/ppermute | solution.py:14
  37.5 4.3 %collective-permute-start = (bf16[2,32,256]{2,1,0:T(8,128)(2,1)S(1)}, bf16[2,32,256]{2,1,0:T(8,128)(2,1)S(1)}, u32[]{:S(2)}, u32[]{:S(2)}) collective-permute-start(bf16[2,32,256]{2,1,0:T(8,128)(2,1)S(1)} %get-tuple-element.434), channel_id=1, source_target_pairs={{7,0},{0,1},{1,2},{2,3},{3,4},{4,5},{5,6},{6,7},{15,8},{8,9},{9,10... | collective-permute-start | bytes 98312 | tf_op jit(solution)/shard_map/while/body/eval_jaxpr/ppermute | solution.py:14
  41.9 4.3 %collective-permute-start = (bf16[2,32,256]{2,1,0:T(8,128)(2,1)S(1)}, bf16[2,32,256]{2,1,0:T(8,128)(2,1)S(1)}, u32[]{:S(2)}, u32[]{:S(2)}) collective-permute-start(bf16[2,32,256]{2,1,0:T(8,128)(2,1)S(1)} %get-tuple-element.434), channel_id=1, source_target_pairs={{7,0},{0,1},{1,2},{2,3},{3,4},{4,5},{5,6},{6,7},{15,8},{8,9},{9,10... | collective-permute-start | bytes 98312 | tf_op jit(solution)/shard_map/while/body/eval_jaxpr/ppermute | solution.py:14
  46.4 4.3 %collective-permute-start = (bf16[2,32,256]{2,1,0:T(8,128)(2,1)S(1)}, bf16[2,32,256]{2,1,0:T(8,128)(2,1)S(1)}, u32[]{:S(2)}, u32[]{:S(2)}) collective-permute-start(bf16[2,32,256]{2,1,0:T(8,128)(2,1)S(1)} %get-tuple-element.434), channel_id=1, source_target_pairs={{7,0},{0,1},{1,2},{2,3},{3,4},{4,5},{5,6},{6,7},{15,8},{8,9},{9,10... | collective-permute-start | bytes 98312 | tf_op jit(solution)/shard_map/while/body/eval_jaxpr/ppermute | solution.py:14
  62.3 30.2 %all-to-all-start = ((bf16[256,32,128]{2,1,0:T(8,128)(2,1)}), bf16[256,32,128]{2,1,0:T(8,128)(2,1)S(1)}, u32[]{:S(2)}, u32[]{:S(2)}) async-start(bf16[256,32,128]{2,1,0:T(8,128)(2,1)} %bitcast.23), calls=%async_computation | async-start | bytes 4194304 | tf_op jit(solution)/shard_map/all_to_all | solution.py:73
  65.9 139.5 %reduce-scatter.2.cloned.1.call-start = ((), (), s32[]{:S(2)}) async-start(), calls=%async_computation.2 | async-start | bytes 294912 | tf_op jit(solution)/shard_map/reduce_scatter | solution.py:113
  65.9 85.9 %collective-permute-start.3 = (bf16[128,32,256]{2,1,0:T(8,128)(2,1)}, bf16[128,32,256]{2,1,0:T(8,128)(2,1)}, u32[]{:S(2)}, u32[]{:S(2)}) collective-permute-start(bf16[128,32,256]{2,1,0:T(8,128)(2,1)} %collective-permute-done.1), channel_id=1, source_target_pairs={{0,8},{8,16},{16,24},{24,0},{1,9},{9,17},{17,25},{25,1},{2,10},{10... | collective-permute-start | bytes 6291464 | tf_op jit(solution)/shard_map/ppermute | solution.py:92
  70.6 4.2 %copy-start.3 = (bf16[128,32,256]{0,2,1:T(8,128)(2,1)S(1)}, bf16[128,32,256]{0,2,1:T(8,128)(2,1)}, u32[]{:S(2)}) copy-start(bf16[128,32,256]{0,2,1:T(8,128)(2,1)} %copy.30) | copy-start | bytes 6291460
  92.5 1.3 copy-start.2
  111.1 3.3 %copy-start.4 = (bf16[128,32,256]{0,2,1:T(8,128)(2,1)S(1)}, bf16[128,32,256]{0,2,1:T(8,128)(2,1)}, u32[]{:S(2)}) copy-start(bf16[128,32,256]{0,2,1:T(8,128)(2,1)} %copy.32) | copy-start | bytes 6291460
  171.5 0.7 copy-start
Sparse Core Ops, SparseCore 0:
  172.3 32.9 reduce-scatter.1
